TPU v7x, 32 devices: a whole 2x2x4 slice. The times are simulated.
32 devices in a mesh: row: 8 (over y, x, core), col: 4 (over z).
Axes of the slice: x: 2, y: 2, z: 4, core: 2. Of those that a mesh axis runs over, the one named last changes fastest.
Arguments:
- queries: bfloat16 [512, 2, 2048], P('row', None, 'col'), may hold values from -15 to 15
- new_keys: bfloat16 [512, 2, 2048], P('row', None, 'col'), may hold values from -6 to 6
- new_values: bfloat16 [512, 2, 2048], P('row', None, 'col'), may hold values from -6 to 6
- cache_keys: bfloat16 [1024, 2, 2048], P('row', None, 'col'), may hold values from -6 to 6
- cache_values: bfloat16 [1024, 2, 2048], P('row', None, 'col'), may hold values from -6 to 6
- cached_len: int32 [2], replicated, may hold values from 256 to 1024, as said below
- residual: bfloat16 [512, 2, 2048], P('row'), may hold values from -4 to 4
- out_weight: bfloat16 [2048, 2048], P('col'), may hold values from -0.125 to 0.125
- norm_gain: float32 [2048], replicated, may hold values from 0.5 to 1.5
- expert_ids: int32 [512, 2, 6], P('row'), may hold values from 0 to 63, all different within a row; in each aligned block of 128 rows (0 to 127, 128 to 255, ..., all dimensions but the last counted through in order) at most 24 rows name the same one
- gate_values: float32 [512, 2, 6], P('row'), may hold values from 0.1 to 0.6
- w_gate: bfloat16 [256, 2048, 352], P(('row', 'col')), may hold values from -0.125 to 0.125
- w_up: bfloat16 [256, 2048, 352], P(('row', 'col')), may hold values from -0.125 to 0.125
- w_down: bfloat16 [256, 352, 2048], P(('row', 'col')), may hold values from -0.15625 to 0.15625
- shared_gate: bfloat16 [2048, 2816], P(None, 'col'), may hold values from -0.125 to 0.125
- shared_up: bfloat16 [2048, 2816], P(None, 'col'), may hold values from -0.125 to 0.125
- shared_down: bfloat16 [2816, 2048], P('col'), may hold values from -0.109375 to 0.109375
Outputs:
- mixed: bfloat16 [512, 2, 2048], P('row', None, 'col')
- ffn_out: bfloat16 [512, 2, 2048], P('row', None, 'col')
Inputs may be any that keep to these rules, and one draw needn't show every extreme that they name: `cached_len`: some request has exactly 1024 cached positions. `expert_ids`: each token names 6 different experts. Among the 128 tokens of one index of row (positions taken in order, requests inside), no expert is named more than 24 times, and in some such blocks one expert is named exactly 24 times.
All inputs are finite; a program needn't handle non-finite values.
Results may differ from a plain program's by a relative error of at most 0.023.
Values may be sent and summed in bfloat16 or wider, within the bound.
No kernel may reach another device: no remote copies, remote signals or barrier semaphores. Data moves between devices by JAX's collectives and lax.ppermute only.
A program may use at most 192 MiB of HBM per device.

v0:
```python
import math
import jax
import jax.numpy as jnp
from jax import lax
from jax.sharding import PartitionSpec as P

HD = 128
E = 64
TOPK = 6
GROUPS = 4
CAP = 24


def body(
    queries,
    new_keys,
    new_values,
    cache_keys,
    cache_values,
    cached_len,
    residual,
    out_weight,
    norm_gain,
    expert_ids,
    gate_values,
    w_gate,
    w_up,
    w_down,
    shared_gate,
    shared_up,
    shared_down,
):
    rows_here = queries.shape[0]
    requests = queries.shape[1]
    heads_here = queries.shape[2] // HD
    cache_rows = cache_keys.shape[0]
    block_rows = cache_rows + rows_here
    model_width = residual.shape[2]
    row_index = lax.axis_index("row")
    row_count = lax.axis_size("row")
    score_scale = 1.0 / math.sqrt(HD)
    keys_here = jnp.concatenate([cache_keys, new_keys], axis=0)
    values_here = jnp.concatenate([cache_values, new_values], axis=0)
    query_heads = queries.reshape(rows_here, requests, heads_here, HD)
    local_pos = row_index * rows_here + jnp.arange(rows_here, dtype=jnp.int32)
    key_piece = lax.all_gather(keys_here, "row", axis=0, tiled=True)
    key_count = key_piece.shape[0]
    global_row = jnp.arange(key_count, dtype=jnp.int32)
    shard_index = global_row // block_rows
    offset_rows = global_row % block_rows
    in_cache = offset_rows < cache_rows
    cache_pos = shard_index * cache_rows + offset_rows
    new_pos = shard_index * rows_here + offset_rows - cache_rows
    cache_ok = in_cache[None, :] & (cache_pos[None, :] < cached_len[:, None])
    new_ok = jnp.logical_not(in_cache)[None, :] & (new_pos[None, :] <= local_pos[:, None])
    allowed = cache_ok[:, None, None, :] | new_ok[None, None, :, :]
    key_heads = key_piece.reshape(key_count, requests, heads_here, HD)
    value_heads = lax.all_gather(values_here, "row", axis=0, tiled=True).reshape(
        key_count, requests, heads_here, HD
    )
    scores = (
        jnp.einsum("irhd,jrhd->rhij", query_heads, key_heads, preferred_element_type=jnp.float32)
        * score_scale
    )
    masked = jnp.where(allowed, scores, -1e30)
    old_max = jnp.full((requests, heads_here, rows_here), -1e30, jnp.float32)
    new_max = jnp.maximum(old_max, jnp.max(masked, axis=-1))
    weights_now = jnp.where(allowed, jnp.exp(masked - new_max[..., None]), 0.0)
    new_sum = jnp.sum(weights_now, axis=-1)
    product = jnp.einsum(
        "rhij,jrhd->rhid",
        weights_now.astype(jnp.bfloat16),
        value_heads,
        preferred_element_type=jnp.float32,
    )
    attended = (product / new_sum[..., None]).astype(jnp.bfloat16)
    head_weights = out_weight.reshape(heads_here, HD, model_width)
    attn_part = jnp.einsum(
        "rhid,hde->ire", attended, head_weights, preferred_element_type=jnp.float32
    )
    attn_full = lax.psum(attn_part.astype(jnp.bfloat16), "col").astype(jnp.float32)
    mixed_full = (residual.astype(jnp.float32) + attn_full).astype(jnp.bfloat16)
    mixed_f32 = mixed_full.astype(jnp.float32)
    normed = (
        mixed_f32
        * lax.rsqrt(jnp.mean(mixed_f32 * mixed_f32, axis=-1, keepdims=True) + 1e-06)
        * norm_gain
    ).astype(jnp.bfloat16)
    token_count = rows_here * requests
    tokens = normed.reshape(token_count, model_width)
    col_index = lax.axis_index("col")
    col_count = lax.axis_size("col")
    entries_here = w_gate.shape[0]
    experts_dev = max(1, entries_here // GROUPS)
    groups_dev = entries_here // experts_dev
    experts_per_row = col_count * entries_here // GROUPS
    slots = row_count * experts_dev * CAP
    chosen = expert_ids.reshape(token_count * TOPK)
    onehot = (chosen[:, None] == jnp.arange(E, dtype=jnp.int32)[None, :]).astype(jnp.int32)
    slot_index = jnp.sum(jnp.cumsum(onehot, axis=0) * onehot, axis=1) - 1
    dest_row = chosen // experts_per_row
    local_expert = chosen - (dest_row * col_count + col_index) * entries_here // GROUPS
    valid = (local_expert >= 0) & (local_expert < experts_dev)
    place = (dest_row * experts_dev + local_expert) * CAP + slot_index
    place = jnp.where(valid, place, -1).reshape(token_count, TOPK)
    hit = place[:, :, None] == jnp.arange(slots, dtype=jnp.int32)[None, None, :]
    dispatch = jnp.sum(hit.astype(jnp.float32), axis=1).astype(jnp.bfloat16)
    combine = jnp.sum(jnp.where(hit, gate_values.reshape(token_count, TOPK, 1), 0.0), axis=1)
    outgoing = lax.dot_general(
        dispatch, tokens, (((0,), (0,)), ((), ())), preferred_element_type=jnp.float32
    ).astype(jnp.bfloat16)
    outgoing = outgoing.reshape(row_count, experts_dev, CAP, model_width)
    arrived = lax.all_to_all(outgoing, "row", 0, 0, tiled=True)
    hidden = w_gate.shape[2]
    wg = w_gate.reshape(experts_dev, groups_dev, model_width, hidden)
    wu = w_up.reshape(experts_dev, groups_dev, model_width, hidden)
    wd = w_down.reshape(experts_dev, groups_dev, hidden, model_width)
    gate_proj = jnp.einsum("nlsd,lgdf->lgnsf", arrived, wg, preferred_element_type=jnp.float32)
    up_proj = jnp.einsum("nlsd,lgdf->lgnsf", arrived, wu, preferred_element_type=jnp.float32)
    hidden_act = (jax.nn.silu(gate_proj) * up_proj).astype(jnp.bfloat16)
    expert_out = jnp.einsum(
        "lgnsf,lgfd->nlsd", hidden_act, wd, preferred_element_type=jnp.float32
    ).astype(jnp.bfloat16)
    returned = lax.all_to_all(expert_out, "row", 0, 0, tiled=True).reshape(slots, model_width)
    combine_hi = combine.astype(jnp.bfloat16)
    combine_lo = (combine - combine_hi.astype(jnp.float32)).astype(jnp.bfloat16)
    routed = jnp.dot(combine_hi, returned, preferred_element_type=jnp.float32) + jnp.dot(
        combine_lo, returned, preferred_element_type=jnp.float32
    )
    shared_g = jnp.dot(tokens, shared_gate, preferred_element_type=jnp.float32)
    shared_u = jnp.dot(tokens, shared_up, preferred_element_type=jnp.float32)
    shared_act = (jax.nn.silu(shared_g) * shared_u).astype(jnp.bfloat16)
    shared_part = jnp.dot(shared_act, shared_down, preferred_element_type=jnp.float32)
    ffn_total = lax.psum_scatter(
        (routed + shared_part).astype(jnp.bfloat16), "col", scatter_dimension=1, tiled=True
    )
    col_width = model_width // col_count
    ffn_here = ffn_total.reshape(rows_here, requests, col_width)
    mixed_here = lax.dynamic_slice_in_dim(mixed_full, col_index * col_width, col_width, 2)
    return (mixed_here, ffn_here)


def solution(mesh):
    in_specs = (
        P("row", None, "col"),
        P("row", None, "col"),
        P("row", None, "col"),
        P("row", None, "col"),
        P("row", None, "col"),
        P(),
        P("row", None, None),
        P("col", None),
        P(),
        P("row", None, None),
        P("row", None, None),
        P(("row", "col"), None, None),
        P(("row", "col"), None, None),
        P(("row", "col"), None, None),
        P(None, "col"),
        P(None, "col"),
        P("col", None),
    )
    out_specs = (P("row", None, "col"), P("row", None, "col"))
    return jax.shard_map(body, mesh=mesh, in_specs=in_specs, out_specs=out_specs, check_vma=False)
```

profile of v0, /device:TPU:0, one launch (start us, length us, event | category | flops | bytes accessed | tf_op | source)
XLA Modules:
  0.0 250.1 jit_solution(14127599166133961431)
XLA Ops:
  7.2 0.0 copy-start
  7.2 0.0 copy-start.7
  7.2 0.0 all-gather.3.cloned.1.call-start
  7.2 2.4 pad_maximum_fusion
  9.7 0.0 all-gather.3.cloned.1.call-update
  9.7 0.0 all-gather.5.cloned.1.call-start
  9.8 2.3 pad_maximum_fusion.1
  12.0 0.0 all-gather.5.cloned.1.call-update
  12.1 0.0 all-reduce.2.cloned.1.call-start
  12.1 0.8 copy.73
  12.9 0.1 eq.44
  13.1 0.1 eq.40
  13.2 1.0 reshape.257
  14.2 1.8 reduce-window.6
  16.0 0.3 slice_reduce_fusion
  16.4 0.1 fusion.38
  16.6 0.0 copy-done.7
  16.6 0.1 compare_and_fusion.1
  16.7 0.1 compare_and_fusion
  16.8 0.1 broadcast_or_fusion
  16.9 28.1 %all-gather.3.cloned.1.call-done = bf16[1536,2,512]{2,1,0:T(2,128)(2,1)} async-done(((bf16[192,2,512]{2,1,0:T(2,128)(2,1)}), bf16[1536,2,512]{2,1,0:T(2,128)(2,1)}) %all-gather.3.cloned.1.call-update) | async-done | bytes 3145744 | tf_op jit(solution)/shard_map/all_gather | solution.py:46
  45.0 8.7 %copy.68 = bf16[1536,2,512]{0,2,1:T(8,128)(2,1)} copy(bf16[1536,2,512]{2,1,0:T(2,128)(2,1)} %all-gather.3.cloned.1.call-done) | data formatting | bytes 6291456 | tf_op jit(solution)/shard_map/all_gather | solution.py:46
  53.7 3.0 %fusion.62 = (f32[2,4,64]{2,1,0:T(4,128)S(1)}, f32[2,4,64,1536]{3,2,1,0:T(8,128)S(1)}) fusion(bf16[1536,2,4,128]{0,3,2,1:T(8,128)(2,1)} %bitcast.114, bf16[64,2,4,128]{3,2,1,0:T(4,128)(2,1)S(1)} %reshape.257, pred[2,64,1536]{2,1,0:T(8,128)(4,1)S(1)} %broadcast_or_fusion), kind=kOutput, calls=%fused_computation.106 | convolution fusion | flops 203685376 | bytes 6621184 | tf_op jit(solution)/shard_map/irhd,jrhd->rhij/dot_general | solution.py:62
  56.7 0.0 copy-start.1
  56.7 1.7 copy-done.1
  58.4 0.8 fusion.3
  59.2 20.0 %all-gather.5.cloned.1.call-done = bf16[1536,2,512]{2,1,0:T(2,128)(2,1)} async-done(((bf16[192,2,512]{2,1,0:T(2,128)(2,1)}), bf16[1536,2,512]{2,1,0:T(2,128)(2,1)}) %all-gather.5.cloned.1.call-update) | async-done | bytes 3145744 | tf_op jit(solution)/shard_map/all_gather | solution.py:58
  79.2 8.7 %copy.71 = bf16[1536,2,512]{0,2,1:T(8,128)(2,1)} copy(bf16[1536,2,512]{2,1,0:T(2,128)(2,1)} %all-gather.5.cloned.1.call-done) | data formatting | bytes 6291456 | tf_op jit(solution)/shard_map/all_gather | solution.py:58
  87.9 5.9 %fusion.11 = bf16[64,2,2048]{2,0,1:T(8,128)(2,1)} fusion(bf16[4,128,2048,1]{2,1,0,3:T(8,128)(2,1)} %bitcast.123, bf16[1536,2,4,128]{0,3,2,1:T(8,128)(2,1)} %bitcast.116, f32[2,4,64,1536]{3,2,1,0:T(8,128)} %copy-done.1, f32[2,4,64]{2,1,0:T(4,128)S(1)} %broadcast_maximum_fusion, pred[2,64,1536]{2,1,0:T(8,128)(4,1)S(1)} %broadcast_or_fusion, ...), kind=kOutput, calls=%fused_computation.21 | convolution fusion | flops 472514560 | bytes 9113600 | tf_op jit(solution)/shard_map/rhid,hde->ire/dot_general | solution.py:78
  93.8 0.0 all-reduce.2.cloned.1.call-update
  93.8 0.1 sub.53
  94.0 0.1 add_select_fusion.2
  94.1 0.1 copy.77
  94.1 0.0 copy-done.6
  94.1 0.1 copy.78
  94.3 0.1 copy.79
  94.3 1.0 select_reduce_fusion
  95.3 37.0 %all-reduce.2.cloned.1.call-done = bf16[64,2,2048]{2,0,1:T(8,128)(2,1)} async-done(((bf16[64,2,2048]{2,0,1:T(8,128)(2,1)}), bf16[64,2,2048]{2,0,1:T(8,128)(2,1)}) %all-reduce.2.cloned.1.call-update) | async-done | bytes 524304 | tf_op jit(solution)/shard_map/psum | solution.py:81
  132.3 1.5 fusion.29
  133.8 0.8 copy-done.2
  134.6 0.0 copy-done.5
  134.6 0.2 fusion.31
  134.8 1.3 copy.80
  136.2 1.2 reshape.262
  137.4 0.6 convolution_convert_fusion
  138.0 24.4 %all_to_all.10 = bf16[8,2,24,2048]{3,2,1,0:T(8,128)(2,1)S(1)} all-to-all(bf16[8,2,24,2048]{3,2,1,0:T(8,128)(2,1)S(1)} %bitcast.115), channel_id=1, replica_groups=mesh['row'=8,'col'=4] {'row'}, dimensions={0} | all-to-all | bytes 3145728 | tf_op jit(solution)/shard_map/all_to_all | solution.py:113
  162.4 8.5 %fusion.17 = f32[2,8,24,4,352]{4,2,3,1,0:T(8,128)} fusion(bf16[2,4,2048,352,1]{2,3,1,4,0:T(8,128)(2,1)} %bitcast.120, bf16[8,2,24,2048]{3,2,1,0:T(8,128)(2,1)S(1)} %all_to_all.10), kind=kOutput, calls=%fused_computation.26 | convolution fusion | flops 2214592512 | bytes 15269888 | tf_op jit(solution)/shard_map/nlsd,lgdf->lgnsf/dot_general | solution.py:119
  171.0 0.0 copy-done.4
  171.0 12.9 %fusion.2 = bf16[8,2,24,2048]{3,2,0,1:T(8,128)(2,1)} fusion(bf16[2,4,352,2048,1]{3,2,1,4,0:T(8,128)(2,1)} %bitcast.121, f32[2,8,24,4,352]{4,2,3,1,0:T(8,128)} %fusion.17, bf16[2,4,2048,352,1]{2,3,1,4,0:T(8,128)(2,1)} %bitcast.122, bf16[8,2,24,2048]{3,2,1,0:T(8,128)(2,1)} %copy-done.4), kind=kOutput, calls=%fused_computation.6 | convolution fusion | flops 4433215488 | bytes 28377088 | tf_op jit(solution)/shard_map/lgnsf,lgfd->nlsd/dot_general | solution.py:121
  183.9 2.7 %copy.83 = bf16[8,2,24,2048]{3,2,1,0:T(8,128)(2,1)} copy(bf16[8,2,24,2048]{3,2,0,1:T(8,128)(2,1)} %fusion.2) | data formatting | bytes 3145728 | tf_op jit(solution)/shard_map/convert_element_type | solution.py:123
  186.6 4.3 %all-to-all-start.1 = ((bf16[8,2,24,2048]{3,2,1,0:T(8,128)(2,1)}), bf16[8,2,24,2048]{3,2,1,0:T(8,128)(2,1)}, u32[]{:S(2)}, u32[]{:S(2)}) async-start(bf16[8,2,24,2048]{3,2,1,0:T(8,128)(2,1)} %copy.83), calls=%async_computation.1 | async-start | bytes 3145728 | tf_op jit(solution)/shard_map/all_to_all | solution.py:124
  190.9 0.0 reduce-scatter.2.cloned.1.call-start
  191.0 3.5 %fusion.63 = f32[128,704]{0,1:T(8,128)} fusion(bf16[128,2048]{1,0:T(8,128)(2,1)S(1)} %reshape.262, bf16[2048,704]{0,1:T(8,128)(2,1)} %param.31), kind=kOutput, calls=%fused_computation.107 | convolution fusion | flops 369098752 | bytes 3768320 | tf_op jit(solution)/shard_map/dot_general | solution.py:130
  194.4 17.5 %all-to-all-done.1 = bf16[8,2,24,2048]{3,2,1,0:T(8,128)(2,1)} async-done(((bf16[8,2,24,2048]{3,2,1,0:T(8,128)(2,1)}), bf16[8,2,24,2048]{3,2,1,0:T(8,128)(2,1)}, u32[]{:S(2)}, u32[]{:S(2)}) %all-to-all-start.1) | async-done | bytes 1572896 | tf_op jit(solution)/shard_map/all_to_all | solution.py:124
  212.0 2.0 fusion.50
  213.9 0.0 copy-done.3
  214.0 2.8 %convolution_add_fusion.1 = f32[128,2048]{1,0:T(8,128)} fusion(f32[128,2048]{1,0:T(8,128)S(1)} %fusion.50, bf16[384,2048]{1,0:T(8,128)(2,1)} %bitcast.28, f32[128,384]{1,0:T(8,128)S(1)} %copy-done.3), kind=kOutput, calls=%fused_computation.10 | convolution fusion | flops 201785344 | bytes 3866624 | tf_op jit(solution)/shard_map/dot_general | solution.py:127
  216.8 0.0 copy-done
  216.8 5.1 %fusion.5 = bf16[128,2048]{1,0:T(8,128)(2,1)} fusion(f32[128,2048]{1,0:T(8,128)} %convolution_add_fusion.1, bf16[704,2048]{1,0:T(8,128)(2,1)S(1)} %copy-done, bf16[128,2048]{1,0:T(8,128)(2,1)S(1)} %reshape.262, bf16[2048,704]{0,1:T(8,128)(2,1)} %param.32, f32[128,704]{0,1:T(8,128)} %fusion.63), kind=kOutput, calls=%fused_computation.12 | convolution fusion | flops 739262464 | bytes 8224768 | tf_op jit(solution)/shard_map/dot_general | solution.py:133
  221.9 0.0 reduce-scatter.2.cloned.1.call-update
  221.9 0.9 constant_dynamic-slice_fusion
  222.9 0.8 copy.84
  223.7 18.3 %reduce-scatter.2.cloned.1.call-done = bf16[128,512]{1,0:T(8,128)(2,1)} async-done(((bf16[128,2048]{1,0:T(8,128)(2,1)}), bf16[128,512]{1,0:T(8,128)(2,1)}) %reduce-scatter.2.cloned.1.call-update) | async-done | bytes 131088 | tf_op jit(solution)/shard_map/reduce_scatter | solution.py:134
  241.9 1.6 reshape.268
  (15 shorter events, 0.1 us)
Async XLA Ops:
  7.2 209.6 %copy-start = (bf16[704,2048]{1,0:T(8,128)(2,1)S(1)}, bf16[704,2048]{1,0:T(8,128)(2,1)}, u32[]{:S(2)}) copy-start(bf16[704,2048]{1,0:T(8,128)(2,1)} %param.33) | copy-start | bytes 8650756
  7.2 9.4 %copy-start.7 = (s32[2]{0:T(128)S(1)}, s32[2]{0:T(128)}, u32[]{:S(2)}) copy-start(s32[2]{0:T(128)} %param.22) | copy-start | bytes 28
  7.2 37.8 %all-gather.3.cloned.1.call-start = ((), (), s32[]{:S(2)}) async-start(), calls=%async_computation.3 | async-start | bytes 3538944 | tf_op jit(solution)/shard_map/all_gather | solution.py:46
  9.7 69.5 %all-gather.5.cloned.1.call-start = ((), (), s32[]{:S(2)}) async-start(), calls=%async_computation.4 | async-start | bytes 3538944 | tf_op jit(solution)/shard_map/all_gather | solution.py:58
  12.1 120.3 %all-reduce.2.cloned.1.call-start = ((), (), s32[]{:S(2)}) async-start(), calls=%async_computation.5 | async-start | bytes 1048576 | tf_op jit(solution)/shard_map/psum | solution.py:81
  56.7 1.7 copy-start.1
  87.9 6.3 %copy-start.6 = (f32[64,2,6]{0,1,2:T(2,128)S(1)}, f32[64,2,6]{0,1,2:T(2,128)}, u32[]{:S(2)}) copy-start(f32[64,2,6]{0,1,2:T(2,128)} %param.27) | copy-start | bytes 9220
  93.8 40.9 %copy-start.5 = (f32[2048]{0:T(1024)S(1)}, f32[2048]{0:T(1024)}, u32[]{:S(2)}) copy-start(f32[2048]{0:T(1024)} %param.25) | copy-start | bytes 24580
  133.8 0.8 copy-start.2
  162.4 8.5 %copy-start.4 = (bf16[8,2,24,2048]{3,2,1,0:T(8,128)(2,1)}, bf16[8,2,24,2048]{3,2,1,0:T(8,128)(2,1)S(1)}, u32[]{:S(2)}) copy-start(bf16[8,2,24,2048]{3,2,1,0:T(8,128)(2,1)S(1)} %all_to_all.10) | copy-start | bytes 4718596
  186.6 25.3 %all-to-all-start.1 = ((bf16[8,2,24,2048]{3,2,1,0:T(8,128)(2,1)}), bf16[8,2,24,2048]{3,2,1,0:T(8,128)(2,1)}, u32[]{:S(2)}, u32[]{:S(2)}) async-start(bf16[8,2,24,2048]{3,2,1,0:T(8,128)(2,1)} %copy.83), calls=%async_computation.1 | async-start | bytes 3145728 | tf_op jit(solution)/shard_map/all_to_all | solution.py:124
  190.9 51.0 %reduce-scatter.2.cloned.1.call-start = ((), (), s32[]{:S(2)}) async-start(), calls=%async_computation.6 | async-start | bytes 655360 | tf_op jit(solution)/shard_map/reduce_scatter | solution.py:134
  212.0 2.0 copy-start.3
Sparse Core Ops, SparseCore 0:
  9.9 35.0 all-gather.2
  46.8 32.3 all-gather.4
  93.9 38.3 all-reduce.1
  222.1 19.8 reduce-scatter.1
where the time goes:
time: 251 us; the launch traced here: 250 us
  waiting for transfers between devices  121 us (48%)
  matrix products  44.3 us (18%)
  local copies, waits for them, and re-layouts  31.3 us (12%)
  blocking collectives  24.4 us (10%)
  between operations  14 us (6%)
  other arithmetic  10.7 us (4%)
  starting transfers between devices  4.45 us (2%)
    psum x1, waiting for transfers between devices, body(): lax.psum(attn_part.astype(jnp.bfloat16), 'col').astype(jnp.float32)  37 us
    all_gather x1, waiting for transfers between devices, body(): key_piece = lax.all_gather(keys_here, 'row', axis=0, tiled=True)  28.1 us
    all_to_all x1, blocking collectives, body(): arrived = lax.all_to_all(outgoing, 'row', 0, 0, tiled=True)  24.4 us
    all_gather x1, waiting for transfers between devices, body(): lax.all_gather(values_here, 'row', axis=0, tiled=True)  20 us
    reduce_scatter x1, waiting for transfers between devices, body(): lax.psum_scatter((routed + shared_part).astype(jnp.bfloat16), 'col', scat...  18.3 us
    all_to_all x1, waiting for transfers between devices, body(): lax.all_to_all(expert_out, 'row', 0, 0, tiled=True)  17.5 us
    dot_general x1, matrix products, body(): jnp.einsum('lgnsf,lgfd->nlsd', hidden_act, wd, preferred_element_type=jnp...  12.9 us
    all_gather x1, local copies, waits for them, and re-layouts, body(): key_piece = lax.all_gather(keys_here, 'row', axis=0, tiled=True)  8.71 us
  transfers between devices with their start and end apart: 5, of which 5 were waited for; matrix products, arithmetic and copies ran while one was open for 10% of the time, Pallas kernels for 0%

commit v1 on v0

--- a/solution.py
+++ b/solution.py
@@ -78,7 +78,9 @@
     attn_part = jnp.einsum(
         "rhid,hde->ire", attended, head_weights, preferred_element_type=jnp.float32
     )
-    attn_full = lax.psum(attn_part.astype(jnp.bfloat16), "col").astype(jnp.float32)
+    attn_full = jnp.sum(lax.all_gather(attn_part.astype(jnp.bfloat16), "col"), axis=0).astype(
+        jnp.float32
+    )
     mixed_full = (residual.astype(jnp.float32) + attn_full).astype(jnp.bfloat16)
     mixed_f32 = mixed_full.astype(jnp.float32)
     normed = (

time: 251 us -> 259 us (1.032)
  waiting for transfers between devices: 121 us -> 127 us
    all_gather x0 -> x1, waiting for transfers between devices: none -> 41.9 us  [body(): lax.all_gather(attn_part.astype(jnp.bfloat16), 'col')]
    psum x1 -> x0, waiting for transfers between devices: 37 us -> none  [body(): lax.psum(attn_part.astype(jnp.bfloat16), 'col').astype(jnp.float32)]
    all_gather x1, waiting for transfers between devices: 28.1 us -> 30.8 us  [body(): key_piece = lax.all_gather(keys_here, 'row', axis=0, tiled=True)]
where the time goes in v1:
time: 259 us; the launch traced here: 258 us
  waiting for transfers between devices  127 us (49%)
  matrix products  44.3 us (17%)
  local copies, waits for them, and re-layouts  30.7 us (12%)
  blocking collectives  24.4 us (9%)
  between operations  14 us (5%)
  other arithmetic  13.2 us (5%)
  starting transfers between devices  4.45 us (2%)
    all_gather x1, waiting for transfers between devices, body(): lax.all_gather(attn_part.astype(jnp.bfloat16), 'col')  41.9 us
    all_gather x1, waiting for transfers between devices, body(): key_piece = lax.all_gather(keys_here, 'row', axis=0, tiled=True)  30.8 us
    all_to_all x1, blocking collectives, body(): arrived = lax.all_to_all(outgoing, 'row', 0, 0, tiled=True)  24.4 us
    all_gather x1, waiting for transfers between devices, body(): lax.all_gather(values_here, 'row', axis=0, tiled=True)  20 us
    all_to_all x1, waiting for transfers between devices, body(): lax.all_to_all(expert_out, 'row', 0, 0, tiled=True)  17.5 us
    reduce_scatter x1, waiting for transfers between devices, body(): lax.psum_scatter((routed + shared_part).astype(jnp.bfloat16), 'col', scat...  17 us
    dot_general x1, matrix products, body(): jnp.einsum('lgnsf,lgfd->nlsd', hidden_act, wd, preferred_element_type=jnp...  12.9 us
    all_gather x1, local copies, waits for them, and re-layouts, body(): key_piece = lax.all_gather(keys_here, 'row', axis=0, tiled=True)  8.71 us
  transfers between devices with their start and end apart: 5, of which 5 were waited for; matrix products, arithmetic and copies ran while one was open for 10% of the time, Pallas kernels for 0%

profile of v1, /device:TPU:0, one launch (start us, length us, event | category | flops | bytes accessed | tf_op | source)
XLA Modules:
  0.0 258.3 jit_solution(4001844207295902741)
XLA Ops:
  7.2 0.0 copy-start
  7.2 0.0 all-gather.5.cloned.1.call-start
  7.2 2.4 pad_maximum_fusion
  9.7 0.0 all-gather.5.cloned.1.call-update
  9.7 0.0 all-gather.7.cloned.1.call-start
  9.7 2.3 pad_maximum_fusion.1
  12.0 0.0 all-gather.7.cloned.1.call-update
  12.0 0.0 all-gather.9.cloned.1.call-start
  12.1 1.0 reshape.257
  13.2 0.7 compare_and_fusion.1
  13.9 0.1 compare_and_fusion
  14.1 0.1 broadcast_or_fusion
  14.2 30.8 %all-gather.5.cloned.1.call-done = bf16[1536,2,512]{2,1,0:T(2,128)(2,1)} async-done(((bf16[192,2,512]{2,1,0:T(2,128)(2,1)}), bf16[1536,2,512]{2,1,0:T(2,128)(2,1)}) %all-gather.5.cloned.1.call-update) | async-done | bytes 3145744 | tf_op jit(solution)/shard_map/all_gather | solution.py:46
  44.9 8.7 %copy.62 = bf16[1536,2,512]{0,2,1:T(8,128)(2,1)} copy(bf16[1536,2,512]{2,1,0:T(2,128)(2,1)} %all-gather.5.cloned.1.call-done) | data formatting | bytes 6291456 | tf_op jit(solution)/shard_map/all_gather | solution.py:46
  53.7 3.0 %fusion.62 = (f32[2,4,64]{2,1,0:T(4,128)S(1)}, f32[2,4,64,1536]{3,2,1,0:T(8,128)S(1)}) fusion(bf16[1536,2,4,128]{0,3,2,1:T(8,128)(2,1)} %bitcast.115, bf16[64,2,4,128]{3,2,1,0:T(4,128)(2,1)S(1)} %reshape.257, pred[2,64,1536]{2,1,0:T(8,128)(4,1)S(1)} %broadcast_or_fusion), kind=kOutput, calls=%fused_computation.106 | convolution fusion | flops 203685376 | bytes 6621184 | tf_op jit(solution)/shard_map/irhd,jrhd->rhij/dot_general | solution.py:62
  56.7 0.0 copy-start.1
  56.7 1.7 copy-done.1
  58.4 0.8 fusion.3
  59.2 20.0 %all-gather.7.cloned.1.call-done = bf16[1536,2,512]{2,1,0:T(2,128)(2,1)} async-done(((bf16[192,2,512]{2,1,0:T(2,128)(2,1)}), bf16[1536,2,512]{2,1,0:T(2,128)(2,1)}) %all-gather.7.cloned.1.call-update) | async-done | bytes 3145744 | tf_op jit(solution)/shard_map/all_gather | solution.py:58
  79.2 8.7 %copy.65 = bf16[1536,2,512]{0,2,1:T(8,128)(2,1)} copy(bf16[1536,2,512]{2,1,0:T(2,128)(2,1)} %all-gather.7.cloned.1.call-done) | data formatting | bytes 6291456 | tf_op jit(solution)/shard_map/all_gather | solution.py:58
  87.9 5.9 %fusion.11 = bf16[64,2,2048]{2,0,1:T(8,128)(2,1)} fusion(bf16[4,128,2048,1]{2,1,0,3:T(8,128)(2,1)} %bitcast.125, bf16[1536,2,4,128]{0,3,2,1:T(8,128)(2,1)} %bitcast.117, f32[2,4,64,1536]{3,2,1,0:T(8,128)} %copy-done.1, f32[2,4,64]{2,1,0:T(4,128)S(1)} %broadcast_maximum_fusion, pred[2,64,1536]{2,1,0:T(8,128)(4,1)S(1)} %broadcast_or_fusion, ...), kind=kOutput, calls=%fused_computation.21 | convolution fusion | flops 472514560 | bytes 9113600 | tf_op jit(solution)/shard_map/rhid,hde->ire/dot_general | solution.py:78
  93.8 0.0 all-gather.9.cloned.1.call-update
  93.8 0.0 copy-done.6
  93.8 0.1 copy.67
  94.0 0.1 eq.44
  94.1 0.1 eq.40
  94.3 0.0 copy-start.5
  94.3 1.8 reduce-window.6
  96.1 0.3 slice_reduce_fusion
  96.4 0.1 fusion.38
  96.6 0.1 sub.53
  96.7 0.1 add_select_fusion.2
  96.8 0.1 copy.71
  96.9 0.0 copy-done.7
  96.9 0.1 copy.72
  97.0 0.1 copy.73
  97.1 1.0 select_reduce_fusion
  98.1 41.9 %all-gather.9.cloned.1.call-done = bf16[256,2,2048]{2,0,1:T(8,128)(2,1)} async-done(((bf16[64,2,2048]{2,0,1:T(8,128)(2,1)}), bf16[256,2,2048]{2,0,1:T(8,128)(2,1)}) %all-gather.9.cloned.1.call-update) | async-done | bytes 2097168 | tf_op jit(solution)/shard_map/all_gather | solution.py:81
  140.0 2.0 reduce_sum.58
  142.0 1.3 fusion.29
  143.4 0.8 copy-done.2
  144.2 0.0 copy-done.5
  144.2 0.2 fusion.31
  144.4 1.3 copy.74
  145.7 1.2 reshape.262
  146.9 0.6 convolution_convert_fusion
  147.5 24.4 %all_to_all.10 = bf16[8,2,24,2048]{3,2,1,0:T(8,128)(2,1)S(1)} all-to-all(bf16[8,2,24,2048]{3,2,1,0:T(8,128)(2,1)S(1)} %bitcast.116), channel_id=1, replica_groups=mesh['row'=8,'col'=4] {'row'}, dimensions={0} | all-to-all | bytes 3145728 | tf_op jit(solution)/shard_map/all_to_all | solution.py:115
  172.0 8.5 %fusion.17 = f32[2,8,24,4,352]{4,2,3,1,0:T(8,128)} fusion(bf16[2,4,2048,352,1]{2,3,1,4,0:T(8,128)(2,1)} %bitcast.122, bf16[8,2,24,2048]{3,2,1,0:T(8,128)(2,1)S(1)} %all_to_all.10), kind=kOutput, calls=%fused_computation.26 | convolution fusion | flops 2214592512 | bytes 15269888 | tf_op jit(solution)/shard_map/nlsd,lgdf->lgnsf/dot_general | solution.py:121
  180.5 0.0 copy-done.4
  180.5 12.9 %fusion.2 = bf16[8,2,24,2048]{3,2,0,1:T(8,128)(2,1)} fusion(bf16[2,4,352,2048,1]{3,2,1,4,0:T(8,128)(2,1)} %bitcast.123, f32[2,8,24,4,352]{4,2,3,1,0:T(8,128)} %fusion.17, bf16[2,4,2048,352,1]{2,3,1,4,0:T(8,128)(2,1)} %bitcast.124, bf16[8,2,24,2048]{3,2,1,0:T(8,128)(2,1)} %copy-done.4), kind=kOutput, calls=%fused_computation.6 | convolution fusion | flops 4433215488 | bytes 28377088 | tf_op jit(solution)/shard_map/lgnsf,lgfd->nlsd/dot_general | solution.py:123
  193.4 2.7 %copy.77 = bf16[8,2,24,2048]{3,2,1,0:T(8,128)(2,1)} copy(bf16[8,2,24,2048]{3,2,0,1:T(8,128)(2,1)} %fusion.2) | data formatting | bytes 3145728 | tf_op jit(solution)/shard_map/convert_element_type | solution.py:125
  196.1 4.3 %all-to-all-start.1 = ((bf16[8,2,24,2048]{3,2,1,0:T(8,128)(2,1)}), bf16[8,2,24,2048]{3,2,1,0:T(8,128)(2,1)}, u32[]{:S(2)}, u32[]{:S(2)}) async-start(bf16[8,2,24,2048]{3,2,1,0:T(8,128)(2,1)} %copy.77), calls=%async_computation.1 | async-start | bytes 3145728 | tf_op jit(solution)/shard_map/all_to_all | solution.py:126
  200.4 0.0 reduce-scatter.2.cloned.1.call-start
  200.5 3.5 %fusion.63 = f32[128,704]{0,1:T(8,128)} fusion(bf16[128,2048]{1,0:T(8,128)(2,1)S(1)} %reshape.262, bf16[2048,704]{0,1:T(8,128)(2,1)} %param.31), kind=kOutput, calls=%fused_computation.107 | convolution fusion | flops 369098752 | bytes 3768320 | tf_op jit(solution)/shard_map/dot_general | solution.py:132
  203.9 17.5 %all-to-all-done.1 = bf16[8,2,24,2048]{3,2,1,0:T(8,128)(2,1)} async-done(((bf16[8,2,24,2048]{3,2,1,0:T(8,128)(2,1)}), bf16[8,2,24,2048]{3,2,1,0:T(8,128)(2,1)}, u32[]{:S(2)}, u32[]{:S(2)}) %all-to-all-start.1) | async-done | bytes 1572896 | tf_op jit(solution)/shard_map/all_to_all | solution.py:126
  221.5 2.0 fusion.50
  223.5 0.0 copy-done.3
  223.5 2.8 %convolution_add_fusion.1 = f32[128,2048]{1,0:T(8,128)} fusion(f32[128,2048]{1,0:T(8,128)S(1)} %fusion.50, bf16[384,2048]{1,0:T(8,128)(2,1)} %bitcast.29, f32[128,384]{1,0:T(8,128)S(1)} %copy-done.3), kind=kOutput, calls=%fused_computation.10 | convolution fusion | flops 201785344 | bytes 3866624 | tf_op jit(solution)/shard_map/dot_general | solution.py:129
  226.3 5.1 %fusion.5 = bf16[128,2048]{1,0:T(8,128)(2,1)} fusion(f32[128,2048]{1,0:T(8,128)} %convolution_add_fusion.1, bf16[704,2048]{1,0:T(8,128)(2,1)S(1)} %copy-done, bf16[128,2048]{1,0:T(8,128)(2,1)S(1)} %reshape.262, bf16[2048,704]{0,1:T(8,128)(2,1)} %param.32, f32[128,704]{0,1:T(8,128)} %fusion.63), kind=kOutput, calls=%fused_computation.12 | convolution fusion | flops 739262464 | bytes 8224768 | tf_op jit(solution)/shard_map/dot_general | solution.py:135
  231.4 0.0 reduce-scatter.2.cloned.1.call-update
  231.5 0.9 constant_dynamic-slice_fusion
  232.4 0.8 copy.78
  233.2 17.0 %reduce-scatter.2.cloned.1.call-done = bf16[128,512]{1,0:T(8,128)(2,1)} async-done(((bf16[128,2048]{1,0:T(8,128)(2,1)}), bf16[128,512]{1,0:T(8,128)(2,1)}) %reduce-scatter.2.cloned.1.call-update) | async-done | bytes 131088 | tf_op jit(solution)/shard_map/reduce_scatter | solution.py:136
  250.2 1.6 reshape.268
  (16 shorter events, 0.1 us)
Async XLA Ops:
  7.2 219.1 %copy-start = (bf16[704,2048]{1,0:T(8,128)(2,1)S(1)}, bf16[704,2048]{1,0:T(8,128)(2,1)}, u32[]{:S(2)}) copy-start(bf16[704,2048]{1,0:T(8,128)(2,1)} %param.33) | copy-start | bytes 8650756
  7.2 37.8 %all-gather.5.cloned.1.call-start = ((), (), s32[]{:S(2)}) async-start(), calls=%async_computation.3 | async-start | bytes 3538944 | tf_op jit(solution)/shard_map/all_gather | solution.py:46
  9.7 69.5 %all-gather.7.cloned.1.call-start = ((), (), s32[]{:S(2)}) async-start(), calls=%async_computation.4 | async-start | bytes 3538944 | tf_op jit(solution)/shard_map/all_gather | solution.py:58
  12.0 127.9 %all-gather.9.cloned.1.call-start = ((), (), s32[]{:S(2)}) async-start(), calls=%async_computation.6 | async-start | bytes 2621440 | tf_op jit(solution)/shard_map/all_gather | solution.py:81
  56.7 1.7 copy-start.1
  87.9 5.9 %copy-start.6 = (s32[64,2,6]{0,1,2:T(2,128)S(1)}, s32[64,2,6]{0,1,2:T(2,128)}, u32[]{:S(2)}) copy-start(s32[64,2,6]{0,1,2:T(2,128)} %param.26) | copy-start | bytes 9220
  87.9 9.0 %copy-start.7 = (f32[64,2,6]{0,1,2:T(2,128)S(1)}, f32[64,2,6]{0,1,2:T(2,128)}, u32[]{:S(2)}) copy-start(f32[64,2,6]{0,1,2:T(2,128)} %param.27) | copy-start | bytes 9220
  94.3 49.9 %copy-start.5 = (f32[2048]{0:T(1024)S(1)}, f32[2048]{0:T(1024)}, u32[]{:S(2)}) copy-start(f32[2048]{0:T(1024)} %param.25) | copy-start | bytes 24580
  143.3 0.8 copy-start.2
  172.0 8.5 %copy-start.4 = (bf16[8,2,24,2048]{3,2,1,0:T(8,128)(2,1)}, bf16[8,2,24,2048]{3,2,1,0:T(8,128)(2,1)S(1)}, u32[]{:S(2)}) copy-start(bf16[8,2,24,2048]{3,2,1,0:T(8,128)(2,1)S(1)} %all_to_all.10) | copy-start | bytes 4718596
  196.1 25.3 %all-to-all-start.1 = ((bf16[8,2,24,2048]{3,2,1,0:T(8,128)(2,1)}), bf16[8,2,24,2048]{3,2,1,0:T(8,128)(2,1)}, u32[]{:S(2)}, u32[]{:S(2)}) async-start(bf16[8,2,24,2048]{3,2,1,0:T(8,128)(2,1)} %copy.77), calls=%async_computation.1 | async-start | bytes 3145728 | tf_op jit(solution)/shard_map/all_to_all | solution.py:126
  200.4 49.8 %reduce-scatter.2.cloned.1.call-start = ((), (), s32[]{:S(2)}) async-start(), calls=%async_computation.5 | async-start | bytes 655360 | tf_op jit(solution)/shard_map/reduce_scatter | solution.py:136
  221.5 2.0 copy-start.3
Sparse Core Ops, SparseCore 0:
  9.9 35.0 all-gather.4
  46.8 32.3 all-gather.6
  94.0 45.9 all-gather.8
  231.6 18.5 reduce-scatter.1
